TPU v7x, 128 devices: a whole 4x4x4 slice. The times are simulated.
128 devices in a mesh: seq: 16 (over y, x_lo, core), tp: 8 (over z, x_hi).
Axes of the slice: x: 4 (x_hi: 2, x_lo: 2; x = x_hi * 2 + x_lo), y: 4, z: 4, core: 2. Of those that a mesh axis runs over, the one named last changes fastest.
Arguments:
- tokens: bfloat16 [8192, 4096], P('seq'), may hold values from -6 to 6
- norm_gain: bfloat16 [4096], replicated, may hold values from 0.099609375 to 1.8984375
- w_query: bfloat16 [4096, 4096], P(None, 'tp'), may hold values from -4 to 4
- w_key: bfloat16 [4096, 512], replicated, may hold values from -1 to 1
- w_value: bfloat16 [4096, 512], replicated, may hold values from -0.09375 to 0.09375
- w_out: bfloat16 [4096, 4096], P('tp'), may hold values from -0.375 to 0.375
- prompt_lengths: int32 [16], replicated, may hold values from 1 to 6144, 8192 in all
- page_slots: int32 [64], replicated, may hold values from 0 to 63, each once
Outputs:
- attended: bfloat16 [8192, 4096], P(('seq', 'tp'))
- kv_cache: bfloat16 [64, 128, 1024], P('seq', None, 'tp')
Inputs may be any that keep to these rules, and one draw needn't show every extreme that they name: `prompt_lengths`: the lengths sum to 8192; the longest prompt has exactly 6144 tokens. `page_slots`: every value appears exactly once.
All inputs are finite; a program needn't handle non-finite values.
Results may differ from a plain program's by a relative error of at most 0.015.
Values may be sent and summed in bfloat16 or wider, within the bound.
No kernel may reach another device: no remote copies, remote signals or barrier semaphores. Data moves between devices by JAX's collectives and lax.ppermute only.
A program may use at most 128 MiB of HBM per device.

v0:
```python
import jax
import jax.numpy as jnp
from jax import lax
from jax.sharding import PartitionSpec as P

HD = 128
PAGE = 128


epsilon = 1e-05
rope_base = 5000000.0


def segment_info(token_index, prompt_lengths):
    prompt_ends = jnp.cumsum(prompt_lengths)
    finished = prompt_ends[None, :] <= token_index[:, None]
    segment = jnp.sum(finished.astype(jnp.int32), axis=1)
    offset = jnp.sum(jnp.where(finished, prompt_lengths[None, :], 0), axis=1)
    return (segment, token_index - offset)


def rotate(vectors, position):
    half_size = HD // 2
    frequency = rope_base ** (-(2.0 * jnp.arange(half_size, dtype=jnp.float32)) / HD)
    angle = position.astype(jnp.float32)[:, None] * frequency[None, :]
    cosine = jnp.cos(angle)[:, None, :]
    sine = jnp.sin(angle)[:, None, :]
    first_half = vectors[..., :half_size]
    second_half = vectors[..., half_size:]
    return jnp.concatenate(
        [first_half * cosine - second_half * sine, second_half * cosine + first_half * sine],
        axis=-1,
    )


def normalize(tokens, norm_gain):
    hidden = tokens.astype(jnp.float32)
    factor = lax.rsqrt(jnp.mean(hidden * hidden, axis=-1, keepdims=True) + epsilon)
    return (hidden * factor * norm_gain.astype(jnp.float32)).astype(jnp.bfloat16)


def attend(
    head_state,
    group_queries,
    group_index,
    group_segment,
    key_rows,
    value_rows,
    key_index,
    key_segment,
):
    running_max, running_sum, weighted = head_state
    scores = jnp.einsum(
        "rhd,nd->hrn", group_queries, key_rows, preferred_element_type=jnp.float32
    ) * HD ** (-0.5)
    visible = (
        (key_index[None, :] <= group_index[:, None])
        & (key_segment[None, :] == group_segment[:, None])
    )[None]
    fresh_max = jnp.maximum(running_max, jnp.max(jnp.where(visible, scores, -1e30), axis=2))
    weights = jnp.where(visible, jnp.exp(scores - fresh_max[..., None]), 0.0)
    shrink = jnp.exp(running_max - fresh_max)
    running_sum = running_sum * shrink + jnp.sum(weights, axis=2)
    weighted = weighted * shrink[..., None] + jnp.einsum(
        "hrn,nd->hrd", weights.astype(jnp.bfloat16), value_rows, preferred_element_type=jnp.float32
    )
    return (fresh_max, running_sum, weighted)


def on_device(tokens, norm_gain, w_query, w_key, w_value, w_out, prompt_lengths, page_slots):
    row_count = tokens.shape[0]
    tp_count = lax.axis_size("tp")
    seq_rank = lax.axis_index("seq")
    tp_rank = lax.axis_index("tp")
    heads_here = w_query.shape[1] // HD
    kv_heads = w_key.shape[1] // HD
    sharing = tp_count // kv_heads
    kv_head = tp_rank // sharing
    token_index = seq_rank * row_count + jnp.arange(row_count, dtype=jnp.int32)
    segment, position = segment_info(token_index, prompt_lengths)
    normed = normalize(tokens, norm_gain)
    queries = rotate(
        jnp.dot(normed, w_query, preferred_element_type=jnp.float32).reshape(
            row_count, heads_here, HD
        ),
        position,
    ).astype(jnp.bfloat16)
    key_columns = lax.dynamic_slice_in_dim(w_key, kv_head * HD, HD, 1)
    value_columns = lax.dynamic_slice_in_dim(w_value, kv_head * HD, HD, 1)
    keys_here = rotate(
        jnp.dot(normed, key_columns, preferred_element_type=jnp.float32)[:, None, :], position
    )[:, 0].astype(jnp.bfloat16)
    values_here = jnp.dot(normed, value_columns, preferred_element_type=jnp.float32).astype(
        jnp.bfloat16
    )
    keys_values = jnp.concatenate([keys_here, values_here], axis=1)
    cache_width = 2 * HD // sharing
    cache_column = tp_rank % sharing * cache_width
    slots_here = row_count // PAGE
    cache_rows = jnp.arange(slots_here * PAGE, dtype=jnp.int32)
    page_total = page_slots.shape[0]
    groups = ((queries, token_index, segment),)

    def step_block(carried, block_input):
        states, cache_here = carried
        block_values, block_start = block_input
        block_size = block_values.shape[0]
        key_index = block_start + jnp.arange(block_size, dtype=jnp.int32)
        key_segment, unused_key_position = segment_info(key_index, prompt_lengths)
        key_rows = block_values[:, :HD]
        value_rows = block_values[:, HD:]
        updated = []
        for head_state, group in zip(states, groups):
            group_queries, group_index, group_segment = group
            head_state = attend(
                head_state,
                group_queries,
                group_index,
                group_segment,
                key_rows,
                value_rows,
                key_index,
                key_segment,
            )
            updated.append(head_state)
        page_number = key_index // PAGE
        global_slot = jnp.sum(
            jnp.where(
                page_number[:, None] == jnp.arange(page_total, dtype=jnp.int32)[None, :],
                page_slots[None, :],
                0,
            ),
            axis=1,
        )
        cache_target = jnp.where(
            global_slot // slots_here == seq_rank,
            global_slot % slots_here * PAGE + key_index % PAGE,
            -1,
        )
        selector = (cache_rows[:, None] == cache_target[None, :]).astype(jnp.bfloat16)
        page_part = lax.dynamic_slice_in_dim(block_values, cache_column, cache_width, 1)
        cache_here = cache_here + jnp.dot(
            selector, page_part, preferred_element_type=jnp.float32
        ).astype(jnp.bfloat16)
        return ((tuple(updated), cache_here), None)

    initial_states = tuple(
        (
            (
                jnp.full((heads_here, group[1].shape[0]), -1e30, jnp.float32),
                jnp.zeros((heads_here, group[1].shape[0]), jnp.float32),
                jnp.zeros((heads_here, group[1].shape[0], HD), jnp.float32),
            )
            for group in groups
        )
    )
    initial_cache = jnp.zeros((slots_here * PAGE, cache_width), jnp.bfloat16)
    carried = (initial_states, initial_cache)
    shard_piece = lax.all_gather(keys_values, "seq", axis=0, tiled=True)
    piece_rows = shard_piece.shape[0]
    block_rows = 512
    blocks = shard_piece.reshape(piece_rows // block_rows, block_rows, 2 * HD)
    block_starts = block_rows * jnp.arange(piece_rows // block_rows, dtype=jnp.int32)
    carried, unused_output = lax.scan(step_block, carried, (blocks, block_starts))
    states, cache_here = carried
    outputs = [
        (weighted / running_sum[..., None])
        .transpose(1, 0, 2)
        .reshape(-1, heads_here * HD)
        .astype(jnp.bfloat16)
        for running_max, running_sum, weighted in states
    ]
    heads_out = outputs[0]
    attended = lax.psum_scatter(
        jnp.dot(heads_out, w_out, preferred_element_type=jnp.float32).astype(jnp.bfloat16),
        "tp",
        scatter_dimension=0,
        tiled=True,
    )
    return (attended, cache_here.reshape(slots_here, PAGE, cache_width))


def solution(mesh):
    placed = (P("seq", None), P(), P(None, "tp"), P(), P(), P("tp", None), P(), P())
    return jax.shard_map(
        on_device,
        mesh=mesh,
        in_specs=placed,
        out_specs=(P(("seq", "tp"), None), P("seq", None, "tp")),
        check_vma=False,
    )
```

profile of v0, /device:TPU:24, one launch (start us, length us, event | category | flops | bytes accessed | tf_op | source)
XLA Modules:
  0.0 305.3 jit_solution(4409422071376044708)
XLA Ops:
  8.1 3.1 %fusion.33 = f32[512]{0:T(512)S(1)} fusion(bf16[512,4096]{1,0:T(8,128)(2,1)} %param.10), kind=kLoop, calls=%fused_computation.59 | loop fusion | flops 6290944 | bytes 4196352 | tf_op jit(solution)/shard_map/reduce_sum | solution.py:38
  11.4 4.2 %convolution_convert_fusion.2 = bf16[512,128]{0,1:T(8,128)(2,1)S(1)} fusion(bf16[4096,512]{1,0:T(8,128)(2,1)} %param.14, s32[]{:T(128)S(6)} %select_n.116, bf16[512,4096]{1,0:T(8,128)(2,1)} %param.10, f32[4096]{0:T(1024)S(1)} %convert_element_type.64, f32[512]{0:T(512)S(1)} %add_rsqrt_fusion), kind=kOutput, calls=%fused_computation.64 | convolution fusion | flops 545325056 | bytes 5392388 | tf_op jit(solution)/shard_map/dot_general | solution.py:93
  15.6 2.8 convolution_bitcast_fusion
  20.1 5.9 %fusion.50 = f32[512,512]{0,1:T(8,128)S(1)} fusion(bf16[4096,512]{1,0:T(8,128)(2,1)} %param.12, bf16[512,4096]{1,0:T(8,128)(2,1)} %param.10, f32[4096]{0:T(1024)S(1)} %convert_element_type.64, f32[512]{0:T(512)S(1)} %add_rsqrt_fusion), kind=kOutput, calls=%fused_computation.96 | convolution fusion | flops 2155872256 | bytes 9455616 | tf_op jit(solution)/shard_map/dot_general | solution.py:83
  26.8 1.0 multiply_cosine_fusion
  28.5 29.8 %all-gather.2.cloned.1.call-done = bf16[8192,256]{0,1:T(8,128)(2,1)} async-done(((bf16[512,256]{0,1:T(8,128)(2,1)}), bf16[8192,256]{0,1:T(8,128)(2,1)}) %all-gather.2.cloned.1.call-update) | async-done | bytes 4194320 | tf_op jit(solution)/shard_map/all_gather | solution.py:159
  58.3 6.4 %copy.25 = bf16[8192,256]{1,0:T(8,128)(2,1)} copy(bf16[8192,256]{0,1:T(8,128)(2,1)} %all-gather.2.cloned.1.call-done) | data formatting | bytes 8388608
  64.7 141.5 %while.20 = (s32[]{:T(128)}, f32[4,512]{1,0:T(4,128)S(1)}, f32[4,512]{1,0:T(4,128)S(1)}, f32[4,512,128]{2,1,0:T(8,128)S(1)}, bf16[512,128]{1,0:T(8,128)(2,1)S(1)...) while((s32[]{:T(128)}, f32[4,512]{1,0:T(4,128)S(1)}, ...), condition=%wide.region_9.10_spmd.clone, body=%wide.region_4.9_spmd.clone.sunk | while | flops 617704960 | bytes 17593384 | solution.py:164
  67.4 1.4 fusion.76
  69.1 1.0 dynamic-slice_bitcast_fusion.2
  72.0 1.5 fusion.75
  76.3 1.4 fusion.76
  78.0 1.0 dynamic-slice_bitcast_fusion.2
  80.8 1.5 fusion.75
  85.1 1.4 fusion.76
  89.7 1.5 fusion.75
  94.0 1.4 fusion.76
  98.5 1.5 fusion.75
  102.8 1.4 fusion.76
  104.5 1.0 dynamic-slice_bitcast_fusion.2
  107.4 1.5 fusion.75
  111.7 1.4 fusion.76
  113.4 1.0 dynamic-slice_bitcast_fusion.2
  116.2 1.5 fusion.75
  120.5 1.4 fusion.76
  125.0 1.5 fusion.75
  129.4 1.4 fusion.76
  131.1 1.0 dynamic-slice_bitcast_fusion.2
  133.9 1.5 fusion.75
  138.2 1.4 fusion.76
  139.9 1.0 dynamic-slice_bitcast_fusion.2
  142.7 1.5 fusion.75
  147.1 1.4 fusion.76
  151.6 1.5 fusion.75
  155.9 1.4 fusion.76
  160.4 1.5 fusion.75
  164.7 1.4 fusion.76
  169.3 1.5 fusion.75
  173.6 1.4 fusion.76
  178.1 1.5 fusion.75
  182.4 1.4 fusion.76
  187.0 1.5 fusion.75
  191.3 1.4 fusion.76
  195.8 1.5 fusion.75
  200.1 1.4 fusion.76
  204.7 1.5 fusion.75
  206.7 6.5 %convolution_convert_fusion.1 = bf16[512,4096]{1,0:T(8,128)(2,1)} fusion(bf16[512,512]{0,1:T(8,128)(2,1)S(1)} %bitcast.68, bf16[512,4096]{1,0:T(8,128)(2,1)} %param.15), kind=kOutput, calls=%fused_computation.62 | convolution fusion | flops 2149580800 | bytes 8912896 | tf_op jit(solution)/shard_map/dot_general | solution.py:175
  213.2 85.3 %reduce-scatter.2.cloned.1.call-done = bf16[64,4096]{1,0:T(8,128)(2,1)} async-done(((bf16[512,4096]{1,0:T(8,128)(2,1)}), bf16[64,4096]{1,0:T(8,128)(2,1)}) %reduce-scatter.2.cloned.1.call-update) | async-done | bytes 524304 | tf_op jit(solution)/shard_map/reduce_scatter | solution.py:174
  (240 shorter events, 91.4 us)
Async XLA Ops:
  7.2 4.1 %copy-start.4 = (s32[16]{0:T(128)S(1)}, s32[16]{0:T(128)}, u32[]{:S(2)}) copy-start(s32[16]{0:T(128)} %param.16) | copy-start | bytes 196
  7.2 4.2 %copy-start.3 = (bf16[4096]{0:T(1024)(128)(2,1)S(1)}, bf16[4096]{0:T(1024)(128)(2,1)}, u32[]{:S(2)}) copy-start(bf16[4096]{0:T(1024)(128)(2,1)} %param.11) | copy-start | bytes 24580
  7.2 51.1 %all-gather.2.cloned.1.call-start = ((), (), s32[]{:S(2)}) async-start(), calls=%async_computation.1 | async-start | bytes 4456448 | tf_op jit(solution)/shard_map/all_gather | solution.py:159
  11.4 4.3 %copy-start = (bf16[512,4096]{1,0:T(8,128)(2,1)S(1)}, bf16[512,4096]{1,0:T(8,128)(2,1)}, u32[]{:S(2)}) copy-start(bf16[512,4096]{1,0:T(8,128)(2,1)} %param.10) | copy-start | bytes 12582916
  19.8 278.7 %reduce-scatter.2.cloned.1.call-start = ((), (), s32[]{:S(2)}) async-start(), calls=%async_computation.2 | async-start | bytes 4718592 | tf_op jit(solution)/shard_map/reduce_scatter | solution.py:174
  28.4 36.2 %copy-start.1 = (f32[4,512,128]{2,1,0:T(8,128)S(1)}, f32[4,512,128]{2,1,0:T(8,128)}, u32[]{:S(2)}) copy-start(f32[4,512,128]{2,1,0:T(8,128)} %custom-call.2) | copy-start | bytes 3145732
  28.5 36.2 %copy-start.2 = (s32[64]{0:T(128)S(1)}, s32[64]{0:T(128)}, u32[]{:S(2)}) copy-start(s32[64]{0:T(128)} %param.17) | copy-start | bytes 772
  206.2 7.0 %copy-start.5 = (bf16[512,128]{1,0:T(8,128)(2,1)}, bf16[512,128]{1,0:T(8,128)(2,1)S(1)}, u32[]{:S(2)}) copy-start(bf16[512,128]{1,0:T(8,128)(2,1)S(1)} %get-tuple-element.271) | copy-start | bytes 393220
Sparse Core Ops, SparseCore 0:
  19.9 38.3 all-gather.1
  213.3 85.0 reduce-scatter.1
where the time goes:
time: 308 us; the launch traced here: 305 us
  waiting for transfers between devices  115 us (37%)
  matrix products  81 us (26%)
  other arithmetic  60.7 us (20%)
  local copies, waits for them, and re-layouts  32.5 us (11%)
  between operations  14.3 us (5%)
    reduce_scatter x1, waiting for transfers between devices, on_device(): lax.psum_scatter(jnp.dot(heads_out, w_out, preferred_element_type=jnp.flo...  85.3 us
    all_gather x1, waiting for transfers between devices, on_device(): shard_piece = lax.all_gather(keys_values, 'seq', axis=0, tiled=True)  29.8 us
    dot_general x16, matrix products, attend(): jnp.einsum('hrn,nd->hrd', weights.astype(jnp.bfloat16), value_rows, prefe...  24.5 us
    dot_general x16, matrix products, step_block(): jnp.dot(selector, page_part, preferred_element_type=jnp.float32)  22.8 us
    squeeze x16, local copies, waits for them, and re-layouts, on_device(): lax.scan(step_block, carried, (blocks, block_starts))  15.6 us
    reduce_sum x16, other arithmetic, attend(): running_sum = running_sum * shrink + jnp.sum(weights, axis=2)  14.5 us
    dot_general x16, matrix products, attend(): jnp.einsum('rhd,nd->hrn', group_queries, key_rows, preferred_element_type...  14.2 us
    select_n x16, other arithmetic, step_block(): jnp.where(global_slot // slots_here == seq_rank, global_slot % slots_here...  10.5 us
  transfers between devices with their start and end apart: 2, of which 2 were waited for; matrix products, arithmetic and copies ran while one was open for 3% of the time, Pallas kernels for 0%

commit v1 on v0

v1 whole, which is shorter than its diff:
```python
import functools

import jax
import jax.numpy as jnp
from jax import lax
from jax.experimental import pallas as pl
from jax.experimental.pallas import tpu as pltpu
from jax.sharding import PartitionSpec as P

HD = 128
PAGE = 128
BQ = 256
BK = 256


epsilon = 1e-05
rope_base = 5000000.0


def segment_start(token_index, prompt_lengths):
    prompt_ends = jnp.cumsum(prompt_lengths)
    finished = prompt_ends[None, :] <= token_index[:, None]
    return jnp.sum(jnp.where(finished, prompt_lengths[None, :], 0), axis=1)


def rotate(vectors, position):
    half_size = HD // 2
    frequency = rope_base ** (-(2.0 * jnp.arange(half_size, dtype=jnp.float32)) / HD)
    angle = position.astype(jnp.float32)[:, None] * frequency[None, :]
    cosine = jnp.cos(angle)[:, None, :]
    sine = jnp.sin(angle)[:, None, :]
    first_half = vectors[..., :half_size]
    second_half = vectors[..., half_size:]
    return jnp.concatenate(
        [first_half * cosine - second_half * sine, second_half * cosine + first_half * sine],
        axis=-1,
    )


def normalize(tokens, norm_gain):
    hidden = tokens.astype(jnp.float32)
    factor = lax.rsqrt(jnp.mean(hidden * hidden, axis=-1, keepdims=True) + epsilon)
    return (hidden * factor * norm_gain.astype(jnp.float32)).astype(jnp.bfloat16)


def flash_kernel(lo_ref, hi_ref, base_ref, q_ref, start_ref, kv_ref, o_ref):
    i = pl.program_id(0)
    q = q_ref[...]
    row_index = base_ref[i] + lax.broadcasted_iota(jnp.int32, (BQ, 1), 0)
    row_start = start_ref[...]
    scale = HD ** (-0.5)

    def body(kb, carry):
        running_max, running_sum, weighted = carry
        offset = pl.multiple_of(kb * BK, BK)
        keys = kv_ref[pl.ds(offset, BK), pl.ds(0, HD)]
        values = kv_ref[pl.ds(offset, BK), pl.ds(HD, HD)]
        scores = lax.dot_general(
            q, keys, (((1,), (1,)), ((), ())), preferred_element_type=jnp.float32
        ) * scale
        key_index = offset + lax.broadcasted_iota(jnp.int32, (1, BK), 1)
        visible = (key_index >= row_start) & (key_index <= row_index)
        fresh_max = jnp.maximum(
            running_max, jnp.max(jnp.where(visible, scores, -1e30), axis=1, keepdims=True)
        )
        weights = jnp.where(visible, jnp.exp(scores - fresh_max), 0.0)
        shrink = jnp.exp(running_max - fresh_max)
        running_sum = running_sum * shrink + jnp.sum(weights, axis=1, keepdims=True)
        weighted = weighted * shrink + jnp.dot(
            weights.astype(jnp.bfloat16), values, preferred_element_type=jnp.float32
        )
        return (fresh_max, running_sum, weighted)

    init = (
        jnp.full((BQ, 1), -1e30, jnp.float32),
        jnp.zeros((BQ, 1), jnp.float32),
        jnp.zeros((BQ, HD), jnp.float32),
    )
    running_max, running_sum, weighted = lax.fori_loop(lo_ref[i], hi_ref[i] + 1, body, init)
    o_ref[...] = (weighted / running_sum).astype(o_ref.dtype)


def flash_attention(queries, row_start, key_values, block_lo, block_hi, block_base):
    rows, width = queries.shape
    heads = width // HD
    q_blocks = rows // BQ
    kv_rows = key_values.shape[0]
    grid_spec = pltpu.PrefetchScalarGridSpec(
        num_scalar_prefetch=3,
        grid=(q_blocks, heads),
        in_specs=[
            pl.BlockSpec((BQ, HD), lambda i, h, lo, hi, base: (i, h)),
            pl.BlockSpec((BQ, 1), lambda i, h, lo, hi, base: (i, 0)),
            pl.BlockSpec((kv_rows, 2 * HD), lambda i, h, lo, hi, base: (0, 0)),
        ],
        out_specs=pl.BlockSpec((BQ, HD), lambda i, h, lo, hi, base: (i, h)),
    )
    return pl.pallas_call(
        flash_kernel,
        grid_spec=grid_spec,
        out_shape=jax.ShapeDtypeStruct((rows, width), jnp.bfloat16),
    )(block_lo, block_hi, block_base, queries, row_start, key_values)


def on_device(tokens, norm_gain, w_query, w_key, w_value, w_out, prompt_lengths, page_slots):
    row_count = tokens.shape[0]
    tp_count = lax.axis_size("tp")
    seq_rank = lax.axis_index("seq")
    tp_rank = lax.axis_index("tp")
    heads_here = w_query.shape[1] // HD
    kv_heads = w_key.shape[1] // HD
    sharing = tp_count // kv_heads
    kv_head = tp_rank // sharing
    token_index = seq_rank * row_count + jnp.arange(row_count, dtype=jnp.int32)
    start = segment_start(token_index, prompt_lengths)
    position = token_index - start
    normed = normalize(tokens, norm_gain)

    key_columns = lax.dynamic_slice_in_dim(w_key, kv_head * HD, HD, 1)
    value_columns = lax.dynamic_slice_in_dim(w_value, kv_head * HD, HD, 1)
    keys_here = rotate(
        jnp.dot(normed, key_columns, preferred_element_type=jnp.float32)[:, None, :], position
    )[:, 0].astype(jnp.bfloat16)
    values_here = jnp.dot(normed, value_columns, preferred_element_type=jnp.float32).astype(
        jnp.bfloat16
    )
    keys_values = jnp.concatenate([keys_here, values_here], axis=1)
    gathered = lax.all_gather(keys_values, "seq", axis=0, tiled=True)

    queries = rotate(
        jnp.dot(normed, w_query, preferred_element_type=jnp.float32).reshape(
            row_count, heads_here, HD
        ),
        position,
    ).astype(jnp.bfloat16).reshape(row_count, heads_here * HD)

    q_blocks = row_count // BQ
    first_rows = start.reshape(q_blocks, BQ)[:, 0]
    block_base = seq_rank * row_count + BQ * jnp.arange(q_blocks, dtype=jnp.int32)
    block_lo = first_rows // BK
    block_hi = (block_base + BQ - 1) // BK
    heads_out = flash_attention(
        queries, start[:, None], gathered, block_lo, block_hi, block_base
    )

    attended = lax.psum_scatter(
        jnp.dot(heads_out, w_out, preferred_element_type=jnp.float32).astype(jnp.bfloat16),
        "tp",
        scatter_dimension=0,
        tiled=True,
    )

    cache_width = 2 * HD // sharing
    cache_column = tp_rank % sharing * cache_width
    slots_here = row_count // PAGE
    page_total = page_slots.shape[0]
    wanted = seq_rank * slots_here + jnp.arange(slots_here, dtype=jnp.int32)
    page_of_slot = jnp.sum(
        jnp.where(
            page_slots[None, :] == wanted[:, None],
            jnp.arange(page_total, dtype=jnp.int32)[None, :],
            0,
        ),
        axis=1,
    )
    pages = [
        lax.dynamic_slice(gathered, (page_of_slot[j] * PAGE, cache_column), (PAGE, cache_width))
        for j in range(slots_here)
    ]
    cache_here = jnp.stack(pages, axis=0)
    return (attended, cache_here)


def solution(mesh):
    placed = (P("seq", None), P(), P(None, "tp"), P(), P(), P("tp", None), P(), P())
    return jax.shard_map(
        on_device,
        mesh=mesh,
        in_specs=placed,
        out_specs=(P(("seq", "tp"), None), P("seq", None, "tp")),
        check_vma=False,
    )
```

time: 308 us -> 257 us (0.83)
  Pallas kernels: 0 us -> 81.9 us
  matrix products: 81 us -> 19.1 us
  other arithmetic: 60.7 us -> 9.71 us
  local copies, waits for them, and re-layouts: 32.5 us -> 4.82 us
  waiting for transfers between devices: 115 us -> 122 us
    pallas_call x0 -> x1, Pallas kernels: none -> 81.9 us  [flash_attention(): pl.pallas_call(flash_kernel, grid_spec=grid_spec, out_shape=jax.ShapeDtyp...]
    dot_general x48 -> x0, matrix products: 61.5 us -> none  [the longest x16 24.5 us: attend(): jnp.einsum('hrn,nd->hrd', weights.astype(jnp.bfloat16), value_rows, prefe...]
    select_n x32 -> x2, other arithmetic: 21 us -> 1.1 us  [the longest x1 0.58 us: on_device(): block_hi = (block_base + BQ - 1) // BK]
    reduce_sum x49 -> x2, other arithmetic: 17.5 us -> 0.27 us  [the longest x1 0.18 us: on_device(): jnp.sum(jnp.where(page_slots[None, :] == wanted[:, None], jnp.arange(page...]
    squeeze x16 -> x0, local copies, waits for them, and re-layouts: 15.6 us -> none  [on_device(): lax.scan(step_block, carried, (blocks, block_starts))]
    add x32 -> x1, other arithmetic: 10.7 us -> 0.01 us  [on_device(): wanted = seq_rank * slots_here + jnp.arange(slots_here, dtype=jnp.int32)]
    reduce_scatter x1, waiting for transfers between devices: 85.3 us -> 95.6 us  [on_device(): lax.psum_scatter(jnp.dot(heads_out, w_out, preferred_element_type=jnp.flo...]
    dynamic_slice x16 -> x0, local copies, waits for them, and re-layouts: 9.38 us -> none  [on_device(): lax.scan(step_block, carried, (blocks, block_starts))]
  transfers between devices with their start and end apart: 2 -> 2, of which waited for: 2 -> 2; matrix products, arithmetic and copies ran while one was open for 3% -> 6% of each run, Pallas kernels for 0% -> 0%
where the time goes in v1:
time: 257 us; the launch traced here: 254 us
  waiting for transfers between devices  122 us (47%)
  Pallas kernels  81.9 us (32%)
  matrix products  19.1 us (7%)
  between operations  16.7 us (6%)
  other arithmetic  9.71 us (4%)
  local copies, waits for them, and re-layouts  4.82 us (2%)
    reduce_scatter x1, waiting for transfers between devices, on_device(): lax.psum_scatter(jnp.dot(heads_out, w_out, preferred_element_type=jnp.flo...  95.6 us
    pallas_call x1, Pallas kernels, flash_attention(): pl.pallas_call(flash_kernel, grid_spec=grid_spec, out_shape=jax.ShapeDtyp...  81.9 us
    all_gather x1, waiting for transfers between devices, on_device(): gathered = lax.all_gather(keys_values, 'seq', axis=0, tiled=True)  26.3 us
    dot_general x1, matrix products, on_device(): jnp.dot(heads_out, w_out, preferred_element_type=jnp.float32)  6.68 us
    dot_general x1, matrix products, on_device(): jnp.dot(normed, w_query, preferred_element_type=jnp.float32)  5.93 us
  transfers between devices with their start and end apart: 2, of which 2 were waited for; matrix products, arithmetic and copies ran while one was open for 6% of the time, Pallas kernels for 0%

profile of v1, /device:TPU:24, one launch (start us, length us, event | category | flops | bytes accessed | tf_op | source)
XLA Modules:
  0.0 254.4 jit_solution(17062003578123898063)
XLA Ops:
  7.2 0.0 copy-start.2
  7.2 0.0 copy-start.1
  7.2 0.0 all-gather.2.cloned.1.call-start
  7.3 3.1 %fusion = f32[512]{0:T(512)S(1)} fusion(bf16[512,4096]{1,0:T(8,128)(2,1)} %param.8), kind=kLoop, calls=%fused_computation.2 | loop fusion | flops 6290944 | bytes 4196352 | tf_op jit(solution)/shard_map/reduce_sum | solution.py:42
  10.4 0.0 copy-done.2
  10.4 0.1 copy.33
  10.5 0.1 reduce
  10.6 0.1 select_reduce_fusion
  10.7 0.0 copy-done.1
  10.8 0.0 copy-start
  10.8 3.9 %convolution_convert_fusion.1 = bf16[512,128]{1,0:T(8,128)(2,1)S(1)} fusion(bf16[4096,512]{1,0:T(8,128)(2,1)} %param.12, s32[]{:T(128)S(6)} %select_n.53, bf16[512,4096]{1,0:T(8,128)(2,1)} %param.8, f32[4096]{0:T(1024)S(1)} %convert_element_type.33, f32[512]{0:T(512)S(1)} %add_rsqrt_fusion), kind=kOutput, calls=%fused_computation.7 | convolution fusion | flops 545325056 | bytes 5392388 | tf_op jit(solution)/shard_map/dot_general | solution.py:124
  14.7 0.0 copy-done
  14.7 2.5 convolution_bitcast_fusion
  17.3 1.2 fusion.10
  18.5 0.1 maximum_bitcast_fusion
  18.6 0.7 pad_maximum_fusion.1
  19.4 0.0 all-gather.2.cloned.1.call-update
  19.4 0.2 reduce-scatter.2.cloned.1.call-start
  19.6 0.8 copy.39.start_ref
  20.5 5.9 %fusion.17 = f32[512,512]{0,1:T(8,128)S(1)} fusion(bf16[4096,512]{1,0:T(8,128)(2,1)} %param.10, bf16[512,4096]{1,0:T(8,128)(2,1)} %param.8, f32[4096]{0:T(1024)S(1)} %convert_element_type.33, f32[512]{0:T(512)S(1)} %add_rsqrt_fusion), kind=kOutput, calls=%fused_computation.52 | convolution fusion | flops 2155872256 | bytes 9455616 | tf_op jit(solution)/shard_map/dot_general | solution.py:131
  26.4 0.1 fusion.19
  26.5 0.4 copy.43
  26.9 0.4 copy.42
  27.3 1.0 multiply_cosine_fusion.1
  28.3 0.6 subtract_convert_fusion
  28.9 0.7 pad_maximum_fusion
  29.6 0.9 copy.46
  30.5 0.6 and_select_fusion
  31.0 0.1 slice_reduce_fusion
  31.2 0.5 and_select_fusion.1.lo_ref
  31.7 26.3 %all-gather.2.cloned.1.call-done.kv_ref = bf16[8192,256]{1,0:T(8,128)(2,1)} async-done(((bf16[512,256]{1,0:T(8,128)(2,1)}), bf16[8192,256]{1,0:T(8,128)(2,1)}) %all-gather.2.cloned.1.call-update) | async-done | bytes 4194320 | tf_op jit(solution)/shard_map/all_gather | solution.py:128
  58.0 81.9 %shard_map.95 = bf16[512,512]{1,0:T(8,128)(2,1)} custom-call(s32[2]{0:T(128)} %and_select_fusion.1.lo_ref, s32[2]{0:T(128)} %get-tuple-element.18.hi_ref, s32[2]{0:T(128)} %get-tuple-element.19.base_ref, bf16[512,512]{1,0:T(8,128)(2,1)} %bitcast.26, s32[512,1]{1,0:T(8,128)} %copy.39.start_ref, bf16[8192,256]{1,0:T(8,128)(2,1)} %all-gather.2.cloned.1.call-done.kv_ref), custom_call_target="tpu_custom_call" | custom-call | tf_op jit(solution)/shard_map/pallas_call | solution.py:98
  139.9 6.7 %convolution_convert_fusion = bf16[512,4096]{1,0:T(8,128)(2,1)} fusion(bf16[512,512]{1,0:T(8,128)(2,1)} %shard_map.95, bf16[512,4096]{1,0:T(8,128)(2,1)} %param.13), kind=kOutput, calls=%fused_computation.5 | convolution fusion | flops 2149580800 | bytes 8912896 | tf_op jit(solution)/shard_map/dot_general | solution.py:147
  146.6 0.0 copy-start.3
  146.6 0.0 reduce-scatter.2.cloned.1.call-update
  146.6 0.6 copy-done.3
  147.2 0.2 select_reduce_fusion.1
  147.4 0.6 fusion.20
  150.5 0.8 dynamic-slice_bitcast_fusion.3
  151.3 0.7 pad_maximum_fusion.2
  152.0 95.6 %reduce-scatter.2.cloned.1.call-done = bf16[64,4096]{1,0:T(8,128)(2,1)} async-done(((bf16[512,4096]{1,0:T(8,128)(2,1)}), bf16[64,4096]{1,0:T(8,128)(2,1)}) %reduce-scatter.2.cloned.1.call-update) | async-done | bytes 524304 | tf_op jit(solution)/shard_map/reduce_scatter | solution.py:146
  (8 shorter events, 0.1 us)
Async XLA Ops:
  7.2 3.2 %copy-start.2 = (s32[16]{0:T(128)S(1)}, s32[16]{0:T(128)}, u32[]{:S(2)}) copy-start(s32[16]{0:T(128)} %param.14) | copy-start | bytes 196
  7.2 3.6 %copy-start.1 = (bf16[4096]{0:T(1024)(128)(2,1)S(1)}, bf16[4096]{0:T(1024)(128)(2,1)}, u32[]{:S(2)}) copy-start(bf16[4096]{0:T(1024)(128)(2,1)} %param.9) | copy-start | bytes 24580
  7.2 50.8 %all-gather.2.cloned.1.call-start = ((), (), s32[]{:S(2)}) async-start(), calls=%async_computation.1 | async-start | bytes 4456448 | tf_op jit(solution)/shard_map/all_gather | solution.py:128
  10.8 4.0 %copy-start = (bf16[512,4096]{1,0:T(8,128)(2,1)S(1)}, bf16[512,4096]{1,0:T(8,128)(2,1)}, u32[]{:S(2)}) copy-start(bf16[512,4096]{1,0:T(8,128)(2,1)} %param.8) | copy-start | bytes 12582916
  19.4 228.2 %reduce-scatter.2.cloned.1.call-start = ((), (), s32[]{:S(2)}) async-start(), calls=%async_computation.2 | async-start | bytes 4718592 | tf_op jit(solution)/shard_map/reduce_scatter | solution.py:146
  146.6 0.7 copy-start.3
Sparse Core Ops, SparseCore 0:
  19.5 38.4 all-gather.1
  146.7 100.7 reduce-scatter.1

commit v2 on v1

--- a/solution.py
+++ b/solution.py
@@ -104,9 +104,9 @@
 
 def on_device(tokens, norm_gain, w_query, w_key, w_value, w_out, prompt_lengths, page_slots):
     row_count = tokens.shape[0]
-    tp_count = lax.axis_size("tp")
+    tp_count = lax.axis_size("tpz") * lax.axis_size("tpx")
     seq_rank = lax.axis_index("seq")
-    tp_rank = lax.axis_index("tp")
+    tp_rank = lax.axis_index("tpz") * lax.axis_size("tpx") + lax.axis_index("tpx")
     heads_here = w_query.shape[1] // HD
     kv_heads = w_key.shape[1] // HD
     sharing = tp_count // kv_heads
@@ -143,12 +143,11 @@
         queries, start[:, None], gathered, block_lo, block_hi, block_base
     )
 
-    attended = lax.psum_scatter(
-        jnp.dot(heads_out, w_out, preferred_element_type=jnp.float32).astype(jnp.bfloat16),
-        "tp",
-        scatter_dimension=0,
-        tiled=True,
+    partial_out = jnp.dot(heads_out, w_out, preferred_element_type=jnp.float32).astype(
+        jnp.bfloat16
     )
+    partial_out = lax.psum_scatter(partial_out, "tpz", scatter_dimension=0, tiled=True)
+    attended = lax.psum_scatter(partial_out, "tpx", scatter_dimension=0, tiled=True)
 
     cache_width = 2 * HD // sharing
     cache_column = tp_rank % sharing * cache_width
@@ -172,11 +171,16 @@
 
 
 def solution(mesh):
-    placed = (P("seq", None), P(), P(None, "tp"), P(), P(), P("tp", None), P(), P())
+    seq_size, tp_size = mesh.devices.shape
+    split_mesh = jax.sharding.Mesh(
+        mesh.devices.reshape(seq_size, tp_size // 2, 2), ("seq", "tpz", "tpx")
+    )
+    tp = ("tpz", "tpx")
+    placed = (P("seq", None), P(), P(None, tp), P(), P(), P(tp, None), P(), P())
     return jax.shard_map(
         on_device,
-        mesh=mesh,
+        mesh=split_mesh,
         in_specs=placed,
-        out_specs=(P(("seq", "tp"), None), P("seq", None, "tp")),
+        out_specs=(P(("seq",) + tp, None), P("seq", None, tp)),
         check_vma=False,
     )

time: 257 us -> 248 us (0.965)
  waiting for transfers between devices: 122 us -> 104 us
  Pallas kernels: 81.9 us -> 89.8 us
    reduce_scatter x1 -> x2, waiting for transfers between devices: 95.6 us -> 77.7 us  [the longest x1 55.7 us: on_device(): lax.psum_scatter(partial_out, 'tpz', scatter_dimension=0, tiled=True)]
    pallas_call x1, Pallas kernels: 81.9 us -> 89.8 us  [flash_attention(): pl.pallas_call(flash_kernel, grid_spec=grid_spec, out_shape=jax.ShapeDtyp...]
  transfers between devices with their start and end apart: 2 -> 3, of which waited for: 2 -> 3; matrix products, arithmetic and copies ran while one was open for 6% -> 6% of each run, Pallas kernels for 0% -> 0%
where the time goes in v2:
time: 248 us; the launch traced here: 244 us
  waiting for transfers between devices  104 us (42%)
  Pallas kernels  89.8 us (36%)
  matrix products  19.1 us (8%)
  between operations  16.5 us (7%)
  other arithmetic  10.3 us (4%)
  local copies, waits for them, and re-layouts  4.3 us (2%)
    pallas_call x1, Pallas kernels, flash_attention(): pl.pallas_call(flash_kernel, grid_spec=grid_spec, out_shape=jax.ShapeDtyp...  89.8 us
    reduce_scatter x1, waiting for transfers between devices, on_device(): lax.psum_scatter(partial_out, 'tpz', scatter_dimension=0, tiled=True)  55.7 us
    all_gather x1, waiting for transfers between devices, on_device(): gathered = lax.all_gather(keys_values, 'seq', axis=0, tiled=True)  26.4 us
    reduce_scatter x1, waiting for transfers between devices, on_device(): lax.psum_scatter(partial_out, 'tpx', scatter_dimension=0, tiled=True)  22 us
    dot_general x1, matrix products, on_device(): jnp.dot(heads_out, w_out, preferred_element_type=jnp.float32)  6.68 us
    dot_general x1, matrix products, on_device(): jnp.dot(normed, w_query, preferred_element_type=jnp.float32)  5.93 us
  transfers between devices with their start and end apart: 3, of which 3 were waited for; matrix products, arithmetic and copies ran while one was open for 6% of the time, Pallas kernels for 0%

profile of v2, /device:TPU:24, one launch (start us, length us, event | category | flops | bytes accessed | tf_op | source)
XLA Modules:
  0.0 244.4 jit_solution(4460469401537026469)
XLA Ops:
  7.2 0.0 copy-start.1
  7.2 0.0 all-gather.2.cloned.1.call-start
  7.3 0.7 convert_element_type.33
  8.0 3.1 %fusion = f32[512]{0:T(512)S(1)} fusion(bf16[512,4096]{1,0:T(8,128)(2,1)} %param.8), kind=kLoop, calls=%fused_computation.2 | loop fusion | flops 6290944 | bytes 4196352 | tf_op jit(solution)/shard_map/reduce_sum | solution.py:42
  11.1 0.0 copy-done.1
  11.1 0.1 copy.33
  11.2 0.1 reduce
  11.3 0.1 select_reduce_fusion
  11.4 0.0 copy-start
  11.4 4.0 %convolution_bitcast_fusion = f32[512,1,128]{2,0,1:T(8,128)S(1)} fusion(bf16[4096,512]{1,0:T(8,128)(2,1)} %param.11, s32[]{:T(128)S(6)} %select_n.53, bf16[512,4096]{1,0:T(8,128)(2,1)} %param.8, f32[4096]{0:T(1024)S(1)} %convert_element_type.33, f32[512]{0:T(512)S(1)} %add_rsqrt_fusion), kind=kOutput, calls=%fused_computation.6 | convolution fusion | flops 545259520 | bytes 5523460 | tf_op jit(solution)/shard_map/dot_general | solution.py:122
  15.4 0.0 copy-done
  15.4 2.6 %convolution_convert_fusion.1 = bf16[512,128]{1,0:T(8,128)(2,1)S(1)} fusion(bf16[4096,512]{1,0:T(8,128)(2,1)} %param.12, s32[]{:T(128)S(6)} %select_n.53, bf16[512,4096]{1,0:T(8,128)(2,1)S(1)} %copy-done, f32[4096]{0:T(1024)S(1)} %convert_element_type.33, f32[512]{0:T(512)S(1)} %add_rsqrt_fusion), kind=kOutput, calls=%fused_computation.7 | convolution fusion | flops 545325056 | bytes 5392388 | tf_op jit(solution)/shard_map/dot_general | solution.py:124
  18.0 1.2 fusion.10
  19.2 0.1 maximum_bitcast_fusion
  19.3 0.7 pad_maximum_fusion.1
  20.0 0.0 all-gather.2.cloned.1.call-update
  20.1 0.2 reduce-scatter.3.cloned.1.call-start
  20.3 5.9 %fusion.17 = f32[512,512]{0,1:T(8,128)S(1)} fusion(bf16[4096,512]{1,0:T(8,128)(2,1)} %param.10, bf16[512,4096]{1,0:T(8,128)(2,1)} %param.8, f32[4096]{0:T(1024)S(1)} %convert_element_type.33, f32[512]{0:T(512)S(1)} %add_rsqrt_fusion), kind=kOutput, calls=%fused_computation.52 | convolution fusion | flops 2155872256 | bytes 9455616 | tf_op jit(solution)/shard_map/dot_general | solution.py:131
  26.3 0.1 fusion.19
  26.3 0.4 copy.42
  26.7 0.4 copy.43
  27.1 1.0 multiply_cosine_fusion.1
  28.1 0.5 subtract_convert_fusion
  28.7 0.7 pad_maximum_fusion
  29.4 0.9 copy.46
  30.3 0.8 copy.39.start_ref
  31.1 0.6 and_select_fusion
  31.7 0.1 slice_reduce_fusion
  31.8 0.5 and_select_fusion.1.lo_ref
  32.3 26.4 %all-gather.2.cloned.1.call-done.kv_ref = bf16[8192,256]{1,0:T(8,128)(2,1)} async-done(((bf16[512,256]{1,0:T(8,128)(2,1)}), bf16[8192,256]{1,0:T(8,128)(2,1)}) %all-gather.2.cloned.1.call-update) | async-done | bytes 4194320 | tf_op jit(solution)/shard_map/all_gather | solution.py:128
  58.7 89.8 %shard_map.95 = bf16[512,512]{1,0:T(8,128)(2,1)} custom-call(s32[2]{0:T(128)} %and_select_fusion.1.lo_ref, s32[2]{0:T(128)} %get-tuple-element.18.hi_ref, s32[2]{0:T(128)} %get-tuple-element.19.base_ref, bf16[512,512]{1,0:T(8,128)(2,1)} %bitcast.26, s32[512,1]{1,0:T(8,128)} %copy.39.start_ref, bf16[8192,256]{1,0:T(8,128)(2,1)} %all-gather.2.cloned.1.call-done.kv_ref), custom_call_target="tpu_custom_call" | custom-call | tf_op jit(solution)/shard_map/pallas_call | solution.py:98
  148.5 6.7 %convolution_convert_fusion = bf16[512,4096]{1,0:T(8,128)(2,1)} fusion(bf16[512,512]{1,0:T(8,128)(2,1)} %shard_map.95, bf16[512,4096]{1,0:T(8,128)(2,1)} %param.13), kind=kOutput, calls=%fused_computation.5 | convolution fusion | flops 2149580800 | bytes 8912896 | tf_op jit(solution)/shard_map/dot_general | solution.py:146
  155.2 0.0 copy-start.2
  155.2 0.0 reduce-scatter.3.cloned.1.call-update
  155.2 0.0 reduce-scatter.5.cloned.1.call-start
  155.3 55.7 %reduce-scatter.3.cloned.1.call-done = bf16[128,4096]{1,0:T(8,128)(2,1)} async-done(((bf16[512,4096]{1,0:T(8,128)(2,1)}), bf16[128,4096]{1,0:T(8,128)(2,1)}) %reduce-scatter.3.cloned.1.call-update) | async-done | bytes 1048592 | tf_op jit(solution)/shard_map/reduce_scatter | solution.py:149
  210.9 0.0 reduce-scatter.5.cloned.1.call-update
  211.0 0.0 copy-done.2
  211.0 0.2 select_reduce_fusion.1
  211.2 0.7 fusion.20
  214.4 0.8 dynamic-slice_bitcast_fusion.3
  215.2 0.7 pad_maximum_fusion.2
  215.9 22.0 %reduce-scatter.5.cloned.1.call-done = bf16[64,4096]{1,0:T(8,128)(2,1)} async-done(((bf16[128,4096]{1,0:T(8,128)(2,1)}), bf16[64,4096]{1,0:T(8,128)(2,1)}) %reduce-scatter.5.cloned.1.call-update) | async-done | bytes 524304 | tf_op jit(solution)/shard_map/reduce_scatter | solution.py:150
  (7 shorter events, 0.1 us)
Async XLA Ops:
  7.2 3.9 %copy-start.1 = (s32[16]{0:T(128)S(1)}, s32[16]{0:T(128)}, u32[]{:S(2)}) copy-start(s32[16]{0:T(128)} %param.14) | copy-start | bytes 196
  7.2 51.5 %all-gather.2.cloned.1.call-start = ((), (), s32[]{:S(2)}) async-start(), calls=%async_computation.2 | async-start | bytes 4456448 | tf_op jit(solution)/shard_map/all_gather | solution.py:128
  11.4 4.0 %copy-start = (bf16[512,4096]{1,0:T(8,128)(2,1)S(1)}, bf16[512,4096]{1,0:T(8,128)(2,1)}, u32[]{:S(2)}) copy-start(bf16[512,4096]{1,0:T(8,128)(2,1)} %param.8) | copy-start | bytes 12582916
  20.1 190.9 %reduce-scatter.3.cloned.1.call-start = ((), (), s32[]{:S(2)}) async-start(), calls=%async_computation.3 | async-start | bytes 5242880 | tf_op jit(solution)/shard_map/reduce_scatter | solution.py:149
  155.2 55.8 %copy-start.2 = (s32[64]{0:T(128)S(1)}, s32[64]{0:T(128)}, u32[]{:S(2)}) copy-start(s32[64]{0:T(128)} %param.15) | copy-start | bytes 772
  155.2 82.7 %reduce-scatter.5.cloned.1.call-start = ((), (), s32[]{:S(2)}) async-start(), calls=%async_computation.4 | async-start | bytes 1572864 | tf_op jit(solution)/shard_map/reduce_scatter | solution.py:150
Sparse Core Ops, SparseCore 0:
  20.2 38.4 all-gather.1
  155.3 55.5 reduce-scatter.2
  214.0 23.8 reduce-scatter.4

commit v3 on v2

--- a/solution.py
+++ b/solution.py
@@ -10,7 +10,7 @@
 HD = 128
 PAGE = 128
 BQ = 256
-BK = 256
+BK = 512
 
 
 epsilon = 1e-05
@@ -43,27 +43,27 @@
     return (hidden * factor * norm_gain.astype(jnp.float32)).astype(jnp.bfloat16)
 
 
-def flash_kernel(lo_ref, hi_ref, base_ref, q_ref, start_ref, kv_ref, o_ref):
+def flash_kernel(lo_ref, hi_ref, base_ref, last_start_ref, q_ref, start_ref, kt_ref, v_ref, o_ref):
     i = pl.program_id(0)
     q = q_ref[...]
     row_index = base_ref[i] + lax.broadcasted_iota(jnp.int32, (BQ, 1), 0)
     row_start = start_ref[...]
     scale = HD ** (-0.5)
 
-    def body(kb, carry):
+    def step(kb, carry, masked):
         running_max, running_sum, weighted = carry
         offset = pl.multiple_of(kb * BK, BK)
-        keys = kv_ref[pl.ds(offset, BK), pl.ds(0, HD)]
-        values = kv_ref[pl.ds(offset, BK), pl.ds(HD, HD)]
-        scores = lax.dot_general(
-            q, keys, (((1,), (1,)), ((), ())), preferred_element_type=jnp.float32
-        ) * scale
-        key_index = offset + lax.broadcasted_iota(jnp.int32, (1, BK), 1)
-        visible = (key_index >= row_start) & (key_index <= row_index)
-        fresh_max = jnp.maximum(
-            running_max, jnp.max(jnp.where(visible, scores, -1e30), axis=1, keepdims=True)
-        )
-        weights = jnp.where(visible, jnp.exp(scores - fresh_max), 0.0)
+        keys_t = kt_ref[:, pl.ds(offset, BK)]
+        values = v_ref[pl.ds(offset, BK), :]
+        scores = jnp.dot(q, keys_t, preferred_element_type=jnp.float32) * scale
+        if masked:
+            key_index = offset + lax.broadcasted_iota(jnp.int32, (1, BK), 1)
+            visible = (key_index >= row_start) & (key_index <= row_index)
+            scores = jnp.where(visible, scores, -1e30)
+        fresh_max = jnp.maximum(running_max, jnp.max(scores, axis=1, keepdims=True))
+        weights = jnp.exp(scores - fresh_max)
+        if masked:
+            weights = jnp.where(visible, weights, 0.0)
         shrink = jnp.exp(running_max - fresh_max)
         running_sum = running_sum * shrink + jnp.sum(weights, axis=1, keepdims=True)
         weighted = weighted * shrink + jnp.dot(
@@ -71,35 +71,46 @@
         )
         return (fresh_max, running_sum, weighted)
 
-    init = (
+    lo = lo_ref[i]
+    hi = hi_ref[i] + 1
+    full_lo = (last_start_ref[i] + BK - 1) // BK
+    full_hi = (base_ref[i] + 1) // BK
+    mid_lo = jnp.minimum(jnp.maximum(full_lo, lo), hi)
+    mid_hi = jnp.maximum(mid_lo, jnp.minimum(full_hi, hi))
+    carry = (
         jnp.full((BQ, 1), -1e30, jnp.float32),
         jnp.zeros((BQ, 1), jnp.float32),
         jnp.zeros((BQ, HD), jnp.float32),
     )
-    running_max, running_sum, weighted = lax.fori_loop(lo_ref[i], hi_ref[i] + 1, body, init)
+    carry = lax.fori_loop(lo, mid_lo, functools.partial(step, masked=True), carry)
+    carry = lax.fori_loop(mid_lo, mid_hi, functools.partial(step, masked=False), carry)
+    carry = lax.fori_loop(mid_hi, hi, functools.partial(step, masked=True), carry)
+    running_max, running_sum, weighted = carry
     o_ref[...] = (weighted / running_sum).astype(o_ref.dtype)
 
 
-def flash_attention(queries, row_start, key_values, block_lo, block_hi, block_base):
+def flash_attention(queries, row_start, keys_t, values, bounds):
     rows, width = queries.shape
     heads = width // HD
     q_blocks = rows // BQ
-    kv_rows = key_values.shape[0]
+    kv_rows = values.shape[0]
+    index = lambda i, h, *_: (i, h)
     grid_spec = pltpu.PrefetchScalarGridSpec(
-        num_scalar_prefetch=3,
+        num_scalar_prefetch=4,
         grid=(q_blocks, heads),
         in_specs=[
-            pl.BlockSpec((BQ, HD), lambda i, h, lo, hi, base: (i, h)),
-            pl.BlockSpec((BQ, 1), lambda i, h, lo, hi, base: (i, 0)),
-            pl.BlockSpec((kv_rows, 2 * HD), lambda i, h, lo, hi, base: (0, 0)),
+            pl.BlockSpec((BQ, HD), index),
+            pl.BlockSpec((BQ, 1), lambda i, h, *_: (i, 0)),
+            pl.BlockSpec((HD, kv_rows), lambda i, h, *_: (0, 0)),
+            pl.BlockSpec((kv_rows, HD), lambda i, h, *_: (0, 0)),
         ],
-        out_specs=pl.BlockSpec((BQ, HD), lambda i, h, lo, hi, base: (i, h)),
+        out_specs=pl.BlockSpec((BQ, HD), index),
     )
     return pl.pallas_call(
         flash_kernel,
         grid_spec=grid_spec,
         out_shape=jax.ShapeDtypeStruct((rows, width), jnp.bfloat16),
-    )(block_lo, block_hi, block_base, queries, row_start, key_values)
+    )(*bounds, queries, row_start, keys_t, values)
 
 
 def on_device(tokens, norm_gain, w_query, w_key, w_value, w_out, prompt_lengths, page_slots):
@@ -124,8 +135,8 @@
     values_here = jnp.dot(normed, value_columns, preferred_element_type=jnp.float32).astype(
         jnp.bfloat16
     )
-    keys_values = jnp.concatenate([keys_here, values_here], axis=1)
-    gathered = lax.all_gather(keys_values, "seq", axis=0, tiled=True)
+    keys_t = lax.all_gather(keys_here.T, "seq", axis=1, tiled=True)
+    values_all = lax.all_gather(values_here, "seq", axis=0, tiled=True)
 
     queries = rotate(
         jnp.dot(normed, w_query, preferred_element_type=jnp.float32).reshape(
@@ -137,10 +148,15 @@
     q_blocks = row_count // BQ
     first_rows = start.reshape(q_blocks, BQ)[:, 0]
     block_base = seq_rank * row_count + BQ * jnp.arange(q_blocks, dtype=jnp.int32)
+    last_rows = start.reshape(q_blocks, BQ)[:, -1]
     block_lo = first_rows // BK
     block_hi = (block_base + BQ - 1) // BK
     heads_out = flash_attention(
-        queries, start[:, None], gathered, block_lo, block_hi, block_base
+        queries,
+        start[:, None],
+        keys_t,
+        values_all,
+        (block_lo, block_hi, block_base, last_rows),
     )
 
     partial_out = jnp.dot(heads_out, w_out, preferred_element_type=jnp.float32).astype(
@@ -149,8 +165,6 @@
     partial_out = lax.psum_scatter(partial_out, "tpz", scatter_dimension=0, tiled=True)
     attended = lax.psum_scatter(partial_out, "tpx", scatter_dimension=0, tiled=True)
 
-    cache_width = 2 * HD // sharing
-    cache_column = tp_rank % sharing * cache_width
     slots_here = row_count // PAGE
     page_total = page_slots.shape[0]
     wanted = seq_rank * slots_here + jnp.arange(slots_here, dtype=jnp.int32)
@@ -162,11 +176,13 @@
         ),
         axis=1,
     )
-    pages = [
-        lax.dynamic_slice(gathered, (page_of_slot[j] * PAGE, cache_column), (PAGE, cache_width))
-        for j in range(slots_here)
-    ]
-    cache_here = jnp.stack(pages, axis=0)
+    key_pages = jnp.stack(
+        [lax.dynamic_slice_in_dim(keys_t, page_of_slot[j] * PAGE, PAGE, 1).T for j in range(slots_here)]
+    )
+    value_pages = jnp.stack(
+        [lax.dynamic_slice_in_dim(values_all, page_of_slot[j] * PAGE, PAGE, 0) for j in range(slots_here)]
+    )
+    cache_here = jnp.where(tp_rank % sharing == 0, key_pages, value_pages)
     return (attended, cache_here)
 
 

time: 248 us -> 228 us (0.919)
  Pallas kernels: 89.8 us -> 52.2 us
  waiting for transfers between devices: 104 us -> 121 us
  local copies, waits for them, and re-layouts: 4.3 us -> 7.01 us
    pallas_call x1, Pallas kernels: 89.8 us -> 52.2 us  [flash_attention(): pl.pallas_call(flash_kernel, grid_spec=grid_spec, out_shape=jax.ShapeDtyp...]
    all_gather x1 -> x2, waiting for transfers between devices: 26.4 us -> 52.6 us  [the longest x1 36.2 us: on_device(): keys_t = lax.all_gather(keys_here.T, 'seq', axis=1, tiled=True)]
    reduce_scatter x1, waiting for transfers between devices: 55.7 us -> 47.8 us  [on_device(): lax.psum_scatter(partial_out, 'tpz', scatter_dimension=0, tiled=True)]
  transfers between devices with their start and end apart: 3 -> 4, of which waited for: 3 -> 4; matrix products, arithmetic and copies ran while one was open for 6% -> 10% of each run, Pallas kernels for 0% -> 0%
where the time goes in v3:
time: 228 us; the launch traced here: 226 us
  waiting for transfers between devices  121 us (53%)
  Pallas kernels  52.2 us (23%)
  matrix products  21.1 us (9%)
  between operations  16.6 us (7%)
  other arithmetic  8.24 us (4%)
  local copies, waits for them, and re-layouts  7.01 us (3%)
    pallas_call x1, Pallas kernels, flash_attention(): pl.pallas_call(flash_kernel, grid_spec=grid_spec, out_shape=jax.ShapeDtyp...  52.2 us
    reduce_scatter x1, waiting for transfers between devices, on_device(): lax.psum_scatter(partial_out, 'tpz', scatter_dimension=0, tiled=True)  47.8 us
    all_gather x1, waiting for transfers between devices, on_device(): keys_t = lax.all_gather(keys_here.T, 'seq', axis=1, tiled=True)  36.2 us
    reduce_scatter x1, waiting for transfers between devices, on_device(): lax.psum_scatter(partial_out, 'tpx', scatter_dimension=0, tiled=True)  20.3 us
    all_gather x1, waiting for transfers between devices, on_device(): values_all = lax.all_gather(values_here, 'seq', axis=0, tiled=True)  16.4 us
    dot_general x1, matrix products, on_device(): jnp.dot(heads_out, w_out, preferred_element_type=jnp.float32)  6.63 us
    dot_general x1, matrix products, on_device(): jnp.dot(normed, w_query, preferred_element_type=jnp.float32)  5.94 us
  transfers between devices with their start and end apart: 4, of which 4 were waited for; matrix products, arithmetic and copies ran while one was open for 10% of the time, Pallas kernels for 0%

profile of v3, /device:TPU:24, one launch (start us, length us, event | category | flops | bytes accessed | tf_op | source)
XLA Modules:
  0.0 226.4 jit_solution(17096916727894956940)
XLA Ops:
  7.2 0.0 copy-start
  7.2 0.0 all-gather.5.cloned.1.call-start
  7.2 3.1 %fusion = f32[512]{0:T(512)S(1)} fusion(bf16[512,4096]{1,0:T(8,128)(2,1)} %param.8), kind=kLoop, calls=%fused_computation.2 | loop fusion | flops 6290944 | bytes 4196352 | tf_op jit(solution)/shard_map/reduce_sum | solution.py:42
  10.3 0.0 copy-done
  10.4 0.0 copy-start.1
  10.4 4.5 %convolution_convert_fusion.1 = bf16[512,128]{1,0:T(8,128)(2,1)} fusion(bf16[4096,512]{1,0:T(8,128)(2,1)} %param.12, s32[]{:T(128)S(6)} %select_n.59, bf16[512,4096]{1,0:T(8,128)(2,1)} %param.8, f32[4096]{0:T(1024)S(1)} %convert_element_type.33, f32[512]{0:T(512)S(1)} %add_rsqrt_fusion), kind=kOutput, calls=%fused_computation.7 | convolution fusion | flops 545325056 | bytes 5392388 | tf_op jit(solution)/shard_map/dot_general | solution.py:135
  14.8 0.0 all-gather.5.cloned.1.call-update
  14.9 0.0 all-gather.3.cloned.1.call-start
  14.9 0.0 copy-done.1
  14.9 0.1 copy.32
  15.0 0.1 reduce
  15.2 0.1 select_reduce_fusion
  15.3 4.1 %convolution_bitcast_fusion = f32[512,1,128]{0,2,1:T(8,128)S(1)} fusion(bf16[4096,512]{1,0:T(8,128)(2,1)} %param.11, s32[]{:T(128)S(6)} %select_n.59, bf16[512,4096]{1,0:T(8,128)(2,1)} %param.8, f32[4096]{0:T(1024)S(1)} %convert_element_type.33, f32[512]{0:T(512)S(1)} %add_rsqrt_fusion), kind=kOutput, calls=%fused_computation.6 | convolution fusion | flops 545259520 | bytes 5523460 | tf_op jit(solution)/shard_map/dot_general | solution.py:133
  19.4 0.6 fusion.10
  20.0 0.7 maximum_bitcast_fusion
  20.6 0.0 all-gather.3.cloned.1.call-update
  20.6 0.2 reduce-scatter.3.cloned.1.call-start
  20.9 0.8 copy.35.start_ref
  21.7 5.9 %fusion.17 = f32[512,512]{0,1:T(8,128)S(1)} fusion(bf16[4096,512]{1,0:T(8,128)(2,1)} %param.10, bf16[512,4096]{1,0:T(8,128)(2,1)} %param.8, f32[4096]{0:T(1024)S(1)} %convert_element_type.33, f32[512]{0:T(512)S(1)} %add_rsqrt_fusion), kind=kOutput, calls=%fused_computation.56 | convolution fusion | flops 2155872256 | bytes 9455616 | tf_op jit(solution)/shard_map/dot_general | solution.py:142
  27.7 0.1 fusion.19
  27.8 0.4 copy.42
  28.2 0.4 copy.41
  28.6 1.0 multiply_cosine_fusion
  29.5 0.6 subtract_convert_fusion
  30.2 0.7 pad_maximum_fusion
  30.9 0.9 copy.45
  31.8 0.5 multiply_add_fusion.base_ref
  32.3 0.8 slice_reduce_fusion
  33.0 0.6 and_select_fusion
  33.6 16.4 %all-gather.5.cloned.1.call-done.v_ref = bf16[8192,128]{1,0:T(8,128)(2,1)} async-done(((bf16[512,128]{1,0:T(8,128)(2,1)}), bf16[8192,128]{1,0:T(8,128)(2,1)}) %all-gather.5.cloned.1.call-update) | async-done | bytes 2097168 | tf_op jit(solution)/shard_map/all_gather | solution.py:139
  50.1 36.2 %all-gather.3.cloned.1.call-done.kt_ref = bf16[128,8192]{1,0:T(8,128)(2,1)} async-done(((bf16[128,512]{1,0:T(8,128)(2,1)}), bf16[128,8192]{1,0:T(8,128)(2,1)}) %all-gather.3.cloned.1.call-update) | async-done | bytes 2097168 | tf_op jit(solution)/shard_map/all_gather | solution.py:138
  86.2 52.2 %shard_map.95 = bf16[512,512]{1,0:T(8,128)(2,1)} custom-call(s32[2]{0:T(128)} %get-tuple-element.33.lo_ref, s32[2]{0:T(128)} %get-tuple-element.32.hi_ref, s32[2]{0:T(128)} %multiply_add_fusion.base_ref, s32[2]{0:T(128)} %get-tuple-element.10.last_start_ref, bf16[512,512]{1,0:T(8,128)(2,1)} %bitcast.44, s32[512,1]{1,0:T(8,128)} %copy.35.start_ref, ...), custom_call_target="tpu_custom_call" | custom-call | tf_op jit(solution)/shard_map/pallas_call | solution.py:109
  138.4 6.6 %convolution_convert_fusion = bf16[512,4096]{1,0:T(8,128)(2,1)} fusion(bf16[512,512]{1,0:T(8,128)(2,1)} %shard_map.95, bf16[512,4096]{1,0:T(8,128)(2,1)} %param.13), kind=kOutput, calls=%fused_computation.5 | convolution fusion | flops 2149580800 | bytes 8912896 | tf_op jit(solution)/shard_map/dot_general | solution.py:162
  145.1 0.0 reduce-scatter.3.cloned.1.call-update
  145.1 0.0 reduce-scatter.5.cloned.1.call-start
  145.2 47.8 %reduce-scatter.3.cloned.1.call-done = bf16[128,4096]{1,0:T(8,128)(2,1)} async-done(((bf16[512,4096]{1,0:T(8,128)(2,1)}), bf16[128,4096]{1,0:T(8,128)(2,1)}) %reduce-scatter.3.cloned.1.call-update) | async-done | bytes 1048592 | tf_op jit(solution)/shard_map/reduce_scatter | solution.py:165
  193.0 0.0 reduce-scatter.5.cloned.1.call-update
  193.0 0.0 copy-done.2
  193.0 0.2 select_reduce_fusion.1
  193.2 0.7 fusion.20
  196.5 0.8 dynamic-slice_bitcast_fusion.3
  197.4 0.1 copy.36
  197.5 0.1 copy.39
  197.6 0.1 copy.38
  197.7 0.1 copy.37
  197.9 0.8 dynamic-slice_bitcast_fusion.7
  198.7 0.8 copy.40
  199.5 20.3 %reduce-scatter.5.cloned.1.call-done = bf16[64,4096]{1,0:T(8,128)(2,1)} async-done(((bf16[128,4096]{1,0:T(8,128)(2,1)}), bf16[64,4096]{1,0:T(8,128)(2,1)}) %reduce-scatter.5.cloned.1.call-update) | async-done | bytes 524304 | tf_op jit(solution)/shard_map/reduce_scatter | solution.py:166
  (10 shorter events, 0.1 us)
Async XLA Ops:
  7.2 3.2 %copy-start = (bf16[4096]{0:T(1024)(128)(2,1)S(1)}, bf16[4096]{0:T(1024)(128)(2,1)}, u32[]{:S(2)}) copy-start(bf16[4096]{0:T(1024)(128)(2,1)} %param.9) | copy-start | bytes 24580
  7.2 42.9 %all-gather.5.cloned.1.call-start = ((), (), s32[]{:S(2)}) async-start(), calls=%async_computation.3 | async-start | bytes 2228224 | tf_op jit(solution)/shard_map/all_gather | solution.py:139
  10.4 4.6 %copy-start.1 = (s32[16]{0:T(128)S(1)}, s32[16]{0:T(128)}, u32[]{:S(2)}) copy-start(s32[16]{0:T(128)} %param.14) | copy-start | bytes 196
  14.9 71.4 %all-gather.3.cloned.1.call-start = ((), (), s32[]{:S(2)}) async-start(), calls=%async_computation.2 | async-start | bytes 2228224 | tf_op jit(solution)/shard_map/all_gather | solution.py:138
  20.6 172.3 %reduce-scatter.3.cloned.1.call-start = ((), (), s32[]{:S(2)}) async-start(), calls=%async_computation.4 | async-start | bytes 5242880 | tf_op jit(solution)/shard_map/reduce_scatter | solution.py:165
  145.1 48.0 %copy-start.2 = (s32[64]{0:T(128)S(1)}, s32[64]{0:T(128)}, u32[]{:S(2)}) copy-start(s32[64]{0:T(128)} %param.15) | copy-start | bytes 772
  145.1 74.7 %reduce-scatter.5.cloned.1.call-start = ((), (), s32[]{:S(2)}) async-start(), calls=%async_computation.5 | async-start | bytes 1572864 | tf_op jit(solution)/shard_map/reduce_scatter | solution.py:166
Sparse Core Ops, SparseCore 0:
  15.0 35.0 all-gather.4
  52.3 33.8 all-gather.2
  145.2 47.7 reduce-scatter.2
  195.9 23.8 reduce-scatter.4

commit v4 on v3

--- a/solution.py
+++ b/solution.py
@@ -9,7 +9,8 @@
 
 HD = 128
 PAGE = 128
-BQ = 256
+BQ = 128
+CHUNKS = 4
 BK = 512
 
 
@@ -43,10 +44,10 @@
     return (hidden * factor * norm_gain.astype(jnp.float32)).astype(jnp.bfloat16)
 
 
-def flash_kernel(lo_ref, hi_ref, base_ref, last_start_ref, q_ref, start_ref, kt_ref, v_ref, o_ref):
+def flash_kernel(lo_ref, hi_ref, base_ref, last_start_ref, q_ref, start_ref, index_ref, kt_ref, kv_ref, o_ref):
     i = pl.program_id(0)
     q = q_ref[...]
-    row_index = base_ref[i] + lax.broadcasted_iota(jnp.int32, (BQ, 1), 0)
+    row_index = index_ref[...]
     row_start = start_ref[...]
     scale = HD ** (-0.5)
 
@@ -54,7 +55,7 @@
         running_max, running_sum, weighted = carry
         offset = pl.multiple_of(kb * BK, BK)
         keys_t = kt_ref[:, pl.ds(offset, BK)]
-        values = v_ref[pl.ds(offset, BK), :]
+        values = kv_ref[pl.ds(offset, BK), pl.ds(HD, HD)]
         scores = jnp.dot(q, keys_t, preferred_element_type=jnp.float32) * scale
         if masked:
             key_index = offset + lax.broadcasted_iota(jnp.int32, (1, BK), 1)
@@ -89,20 +90,22 @@
     o_ref[...] = (weighted / running_sum).astype(o_ref.dtype)
 
 
-def flash_attention(queries, row_start, keys_t, values, bounds):
+def flash_attention(queries, row_start, row_index, keys_t, key_values, bounds):
     rows, width = queries.shape
     heads = width // HD
     q_blocks = rows // BQ
-    kv_rows = values.shape[0]
+    kv_rows = key_values.shape[0]
     index = lambda i, h, *_: (i, h)
+    rows_of = lambda i, h, *_: (i, 0)
     grid_spec = pltpu.PrefetchScalarGridSpec(
         num_scalar_prefetch=4,
         grid=(q_blocks, heads),
         in_specs=[
             pl.BlockSpec((BQ, HD), index),
-            pl.BlockSpec((BQ, 1), lambda i, h, *_: (i, 0)),
+            pl.BlockSpec((BQ, 1), rows_of),
+            pl.BlockSpec((BQ, 1), rows_of),
             pl.BlockSpec((HD, kv_rows), lambda i, h, *_: (0, 0)),
-            pl.BlockSpec((kv_rows, HD), lambda i, h, *_: (0, 0)),
+            pl.BlockSpec((kv_rows, 2 * HD), lambda i, h, *_: (0, 0)),
         ],
         out_specs=pl.BlockSpec((BQ, HD), index),
     )
@@ -110,7 +113,7 @@
         flash_kernel,
         grid_spec=grid_spec,
         out_shape=jax.ShapeDtypeStruct((rows, width), jnp.bfloat16),
-    )(*bounds, queries, row_start, keys_t, values)
+    )(*bounds, queries, row_start, row_index, keys_t, key_values)
 
 
 def on_device(tokens, norm_gain, w_query, w_key, w_value, w_out, prompt_lengths, page_slots):
@@ -135,8 +138,9 @@
     values_here = jnp.dot(normed, value_columns, preferred_element_type=jnp.float32).astype(
         jnp.bfloat16
     )
-    keys_t = lax.all_gather(keys_here.T, "seq", axis=1, tiled=True)
-    values_all = lax.all_gather(values_here, "seq", axis=0, tiled=True)
+    keys_values = jnp.concatenate([keys_here, values_here], axis=1)
+    gathered = lax.all_gather(keys_values, "seq", axis=0, tiled=True)
+    keys_t = gathered[:, :HD].T
 
     queries = rotate(
         jnp.dot(normed, w_query, preferred_element_type=jnp.float32).reshape(
@@ -145,26 +149,28 @@
         position,
     ).astype(jnp.bfloat16).reshape(row_count, heads_here * HD)
 
-    q_blocks = row_count // BQ
-    first_rows = start.reshape(q_blocks, BQ)[:, 0]
-    block_base = seq_rank * row_count + BQ * jnp.arange(q_blocks, dtype=jnp.int32)
-    last_rows = start.reshape(q_blocks, BQ)[:, -1]
-    block_lo = first_rows // BK
-    block_hi = (block_base + BQ - 1) // BK
-    heads_out = flash_attention(
-        queries,
-        start[:, None],
-        keys_t,
-        values_all,
-        (block_lo, block_hi, block_base, last_rows),
-    )
-
-    partial_out = jnp.dot(heads_out, w_out, preferred_element_type=jnp.float32).astype(
-        jnp.bfloat16
-    )
-    partial_out = lax.psum_scatter(partial_out, "tpz", scatter_dimension=0, tiled=True)
-    attended = lax.psum_scatter(partial_out, "tpx", scatter_dimension=0, tiled=True)
-
+    piece = row_count // tp_count // CHUNKS
+    chunk_queries = queries.reshape(tp_count, CHUNKS, piece, heads_here * HD)
+    chunk_start = start.reshape(tp_count, CHUNKS, piece)
+    chunk_index = token_index.reshape(tp_count, CHUNKS, piece)
+    outputs = []
+    for c in range(CHUNKS):
+        q_rows = chunk_queries[:, c].reshape(tp_count * piece, heads_here * HD)
+        s_rows = chunk_start[:, c].reshape(tp_count * piece)
+        i_rows = chunk_index[:, c].reshape(tp_count * piece)
+        bounds = (s_rows[:1] // BK, i_rows[-1:] // BK, i_rows[:1], s_rows[-1:])
+        heads_out = flash_attention(
+            q_rows, s_rows[:, None], i_rows[:, None], keys_t, gathered, bounds
+        )
+        partial_out = jnp.dot(heads_out, w_out, preferred_element_type=jnp.float32).astype(
+            jnp.bfloat16
+        )
+        partial_out = lax.psum_scatter(partial_out, "tpz", scatter_dimension=0, tiled=True)
+        outputs.append(lax.psum_scatter(partial_out, "tpx", scatter_dimension=0, tiled=True))
+    attended = jnp.stack(outputs, axis=0).reshape(-1, outputs[0].shape[1])
+
+    cache_width = 2 * HD // sharing
+    cache_column = tp_rank % sharing * cache_width
     slots_here = row_count // PAGE
     page_total = page_slots.shape[0]
     wanted = seq_rank * slots_here + jnp.arange(slots_here, dtype=jnp.int32)
@@ -176,13 +182,11 @@
         ),
         axis=1,
     )
-    key_pages = jnp.stack(
-        [lax.dynamic_slice_in_dim(keys_t, page_of_slot[j] * PAGE, PAGE, 1).T for j in range(slots_here)]
-    )
-    value_pages = jnp.stack(
-        [lax.dynamic_slice_in_dim(values_all, page_of_slot[j] * PAGE, PAGE, 0) for j in range(slots_here)]
-    )
-    cache_here = jnp.where(tp_rank % sharing == 0, key_pages, value_pages)
+    pages = [
+        lax.dynamic_slice(gathered, (page_of_slot[j] * PAGE, cache_column), (PAGE, cache_width))
+        for j in range(slots_here)
+    ]
+    cache_here = jnp.stack(pages, axis=0)
     return (attended, cache_here)
 
 

time: 228 us -> 316 us (1.39)
  Pallas kernels: 52.2 us -> 108 us
  between operations: 16.6 us -> 37.1 us
  local copies, waits for them, and re-layouts: 7.01 us -> 17.7 us
  waiting for transfers between devices: 121 us -> 111 us
  matrix products: 21.1 us -> 28.4 us
    pallas_call x1 -> x4, Pallas kernels: 52.2 us -> 108 us  [flash_attention(): pl.pallas_call(flash_kernel, grid_spec=grid_spec, out_shape=jax.ShapeDtyp...]
    reduce_scatter x1 -> x4, waiting for transfers between devices: 20.3 us -> 65.4 us  [on_device(): lax.psum_scatter(partial_out, 'tpx', scatter_dimension=0, tiled=True)]
    all_gather x2 -> x1, waiting for transfers between devices: 52.6 us -> 20.8 us  [on_device(): gathered = lax.all_gather(keys_values, 'seq', axis=0, tiled=True)]
    reduce_scatter x1 -> x4, waiting for transfers between devices: 47.8 us -> 22.6 us  [on_device(): lax.psum_scatter(partial_out, 'tpz', scatter_dimension=0, tiled=True)]
    dot_general x1 -> x4, matrix products: 6.63 us -> 16 us  [on_device(): jnp.dot(heads_out, w_out, preferred_element_type=jnp.float32)]
    another operation x7 -> x18, local copies, waits for them, and re-layouts: 2.22 us -> 7.8 us  [the longest x4 2.8 us: on_device(): i_rows[:, None]]
    transpose x0 -> x2, local copies, waits for them, and re-layouts: none -> 4.72 us  [on_device(): keys_t = gathered[:, :HD].T]
    another operation x4 -> x6, other arithmetic: 1.33 us -> 4.62 us
  transfers between devices with their start and end apart: 4 -> 9, of which waited for: 4 -> 6; matrix products, arithmetic and copies ran while one was open for 10% -> 11% of each run, Pallas kernels for 0% -> 26%
where the time goes in v4:
time: 316 us; the launch traced here: 314 us
  waiting for transfers between devices  111 us (35%)
  Pallas kernels  108 us (34%)
  between operations  37.1 us (12%)
  matrix products  28.4 us (9%)
  local copies, waits for them, and re-layouts  17.7 us (6%)
  other arithmetic  11.3 us (4%)
    pallas_call x4, Pallas kernels, flash_attention(): pl.pallas_call(flash_kernel, grid_spec=grid_spec, out_shape=jax.ShapeDtyp...  108 us
    reduce_scatter x4, waiting for transfers between devices, on_device(): lax.psum_scatter(partial_out, 'tpx', scatter_dimension=0, tiled=True)  65.4 us
    reduce_scatter x4, waiting for transfers between devices, on_device(): lax.psum_scatter(partial_out, 'tpz', scatter_dimension=0, tiled=True)  22.6 us
    all_gather x1, waiting for transfers between devices, on_device(): gathered = lax.all_gather(keys_values, 'seq', axis=0, tiled=True)  20.8 us
    dot_general x4, matrix products, on_device(): jnp.dot(heads_out, w_out, preferred_element_type=jnp.float32)  16 us
  transfers between devices with their start and end apart: 9, of which 6 were waited for; matrix products, arithmetic and copies ran while one was open for 11% of the time, Pallas kernels for 26%

profile of v4, /device:TPU:24, one launch (start us, length us, event | category | flops | bytes accessed | tf_op | source)
XLA Modules:
  0.0 313.9 jit_solution(829073804654254171)
XLA Ops:
  7.3 0.7 copy.59
  8.2 0.7 convert_element_type.42
  8.9 3.1 fusion
  12.1 3.9 %convolution_convert_fusion.4 = bf16[512,128]{1,0:T(8,128)(2,1)S(1)} fusion(bf16[4096,512]{1,0:T(8,128)(2,1)} %param.12, s32[]{:T(128)S(6)} %select_n.71, bf16[512,4096]{1,0:T(8,128)(2,1)} %param.8, f32[4096]{0:T(1024)S(1)} %convert_element_type.42, f32[512]{0:T(512)S(1)} %add_rsqrt_fusion), kind=kOutput, calls=%fused_computation.11 | convolution fusion | flops 545325056 | bytes 5392388 | tf_op jit(solution)/shard_map/dot_general | solution.py:138
  16.0 2.6 convolution_bitcast_fusion
  18.6 1.2 fusion.10
  19.9 0.7 pad_maximum_fusion.2
  21.3 0.6 fusion.29
  26.9 0.7 broadcast_in_dim_reshape_squeeze.39.index_ref
  27.6 5.9 %fusion.17 = f32[512,512]{0,1:T(8,128)S(1)} fusion(bf16[4096,512]{1,0:T(8,128)(2,1)} %param.10, bf16[512,4096]{1,0:T(8,128)(2,1)} %param.8, f32[4096]{0:T(1024)S(1)} %convert_element_type.42, f32[512]{0:T(512)S(1)} %add_rsqrt_fusion), kind=kOutput, calls=%fused_computation.51 | convolution fusion | flops 2155872256 | bytes 9455616 | tf_op jit(solution)/shard_map/dot_general | solution.py:146
  33.7 0.4 copy.80
  34.5 1.0 multiply_cosine_fusion.1
  35.5 0.6 subtract_convert_fusion
  36.1 0.7 pad_maximum_fusion
  37.0 0.7 broadcast_in_dim_reshape_squeeze.38.start_ref
  37.7 0.8 fusion.20
  38.5 20.8 %all-gather.2.cloned.1.call-done.kv_ref = bf16[8192,256]{1,0:T(8,128)(2,1)} async-done(((bf16[512,256]{1,0:T(8,128)(2,1)}), bf16[8192,256]{1,0:T(8,128)(2,1)}) %all-gather.2.cloned.1.call-update) | async-done | bytes 4194320 | tf_op jit(solution)/shard_map/all_gather | solution.py:142
  59.3 1.7 slice_bitcast_fusion
  61.0 3.0 copy.67.kt_ref
  64.0 26.9 %shard_map.98 = bf16[128,512]{1,0:T(8,128)(2,1)} custom-call(s32[1]{0:T(128)S(6)} %select_n.76.lo_ref, s32[1]{0:T(128)S(6)} %select_n.77.hi_ref, s32[1]{0:T(128)} %get-tuple-element.51.base_ref, s32[1]{0:T(128)} %get-tuple-element.46.last_start_ref, bf16[128,512]{1,0:T(8,128)(2,1)} %bitcast.63, s32[128,1]{1,0:T(8,128)} %broadcast_in_dim_reshape_squeeze.38.start_ref, ...), custom_call_target="tpu_custom_call" | custom-call | tf_op jit(solution)/shard_map/pallas_call | solution.py:112
  90.9 4.0 %convolution_convert_fusion = bf16[128,4096]{1,0:T(8,128)(2,1)} fusion(bf16[128,512]{1,0:T(8,128)(2,1)} %shard_map.98, bf16[512,4096]{1,0:T(8,128)(2,1)} %param.13), kind=kOutput, calls=%fused_computation.5 | convolution fusion | flops 537395200 | bytes 5373952 | tf_op jit(solution)/shard_map/dot_general | solution.py:165
  95.1 0.6 fusion.27
  100.8 0.7 broadcast_in_dim_reshape_squeeze.37.index_ref
  101.5 0.7 broadcast_in_dim_reshape_squeeze.36.start_ref
  102.2 27.0 %shard_map.97 = bf16[128,512]{1,0:T(8,128)(2,1)} custom-call(s32[1]{0:T(128)S(6)} %select_n.74.lo_ref, s32[1]{0:T(128)S(6)} %select_n.75.hi_ref, s32[1]{0:T(128)} %get-tuple-element.53.base_ref, s32[1]{0:T(128)} %get-tuple-element.42.last_start_ref, bf16[128,512]{1,0:T(8,128)(2,1)} %bitcast.62, s32[128,1]{1,0:T(8,128)} %broadcast_in_dim_reshape_squeeze.36.start_ref, ...), custom_call_target="tpu_custom_call" | custom-call | tf_op jit(solution)/shard_map/pallas_call | solution.py:112
  129.2 4.0 %convolution_convert_fusion.1 = bf16[128,4096]{1,0:T(8,128)(2,1)} fusion(bf16[128,512]{1,0:T(8,128)(2,1)} %shard_map.97, bf16[512,4096]{1,0:T(8,128)(2,1)} %param.13), kind=kOutput, calls=%fused_computation.6 | convolution fusion | flops 537395200 | bytes 5373952 | tf_op jit(solution)/shard_map/dot_general | solution.py:165
  133.4 0.7 fusion.25
  139.4 0.7 broadcast_in_dim_reshape_squeeze.35.index_ref
  140.1 0.7 broadcast_in_dim_reshape_squeeze.34.start_ref
  140.8 27.0 %shard_map.96 = bf16[128,512]{1,0:T(8,128)(2,1)} custom-call(s32[1]{0:T(128)S(6)} %select_n.72.lo_ref, s32[1]{0:T(128)S(6)} %select_n.73.hi_ref, s32[1]{0:T(128)} %get-tuple-element.55.base_ref, s32[1]{0:T(128)} %get-tuple-element.38.last_start_ref, bf16[128,512]{1,0:T(8,128)(2,1)} %bitcast.61, s32[128,1]{1,0:T(8,128)} %broadcast_in_dim_reshape_squeeze.34.start_ref, ...), custom_call_target="tpu_custom_call" | custom-call | tf_op jit(solution)/shard_map/pallas_call | solution.py:112
  167.8 4.1 %convolution_convert_fusion.2 = bf16[128,4096]{1,0:T(8,128)(2,1)} fusion(bf16[128,512]{1,0:T(8,128)(2,1)} %shard_map.96, bf16[512,4096]{1,0:T(8,128)(2,1)} %param.13), kind=kOutput, calls=%fused_computation.7 | convolution fusion | flops 537395200 | bytes 5373952 | tf_op jit(solution)/shard_map/dot_general | solution.py:165
  172.3 0.7 fusion.23
  178.1 0.7 broadcast_in_dim_reshape_squeeze.33.index_ref
  178.8 0.7 broadcast_in_dim_reshape_squeeze.32.start_ref
  179.5 27.0 %shard_map.95 = bf16[128,512]{1,0:T(8,128)(2,1)} custom-call(s32[1]{0:T(128)S(6)} %select_n.68.lo_ref, s32[1]{0:T(128)S(6)} %select_n.69.hi_ref, s32[1]{0:T(128)} %get-tuple-element.57.base_ref, s32[1]{0:T(128)} %get-tuple-element.34.last_start_ref, bf16[128,512]{1,0:T(8,128)(2,1)} %bitcast.60, s32[128,1]{1,0:T(8,128)} %broadcast_in_dim_reshape_squeeze.32.start_ref, ...), custom_call_target="tpu_custom_call" | custom-call | tf_op jit(solution)/shard_map/pallas_call | solution.py:112
  206.5 4.0 %convolution_convert_fusion.3 = bf16[128,4096]{1,0:T(8,128)(2,1)} fusion(bf16[128,512]{1,0:T(8,128)(2,1)} %shard_map.95, bf16[512,4096]{1,0:T(8,128)(2,1)} %param.13), kind=kOutput, calls=%fused_computation.8 | convolution fusion | flops 537395200 | bytes 5373952 | tf_op jit(solution)/shard_map/dot_general | solution.py:165
  210.6 0.5 reduce-scatter.23.cloned.1.call-update
  211.2 0.7 reduce-scatter.19.cloned.1.call-update
  211.9 0.7 reduce-scatter.15.cloned.1.call-update
  212.6 22.6 %reduce-scatter.9.cloned.1.call-done = bf16[32,4096]{1,0:T(8,128)(2,1)} async-done(((bf16[128,4096]{1,0:T(8,128)(2,1)}), bf16[32,4096]{1,0:T(8,128)(2,1)}) %reduce-scatter.9.cloned.1.call-update) | async-done | bytes 262160 | tf_op jit(solution)/shard_map/reduce_scatter | solution.py:168
  235.4 0.6 fusion.22
  238.5 0.8 dynamic-slice_bitcast_fusion.3
  239.4 0.7 pad_maximum_fusion.3
  240.1 12.7 %reduce-scatter.23.cloned.1.call-done = bf16[16,4096]{1,0:T(8,128)(2,1)} async-done(((bf16[32,4096]{1,0:T(8,128)(2,1)}), bf16[16,4096]{1,0:T(8,128)(2,1)}) %reduce-scatter.23.cloned.1.call-update) | async-done | bytes 131088 | tf_op jit(solution)/shard_map/reduce_scatter | solution.py:169
  252.7 17.6 %reduce-scatter.19.cloned.1.call-done = bf16[16,4096]{1,0:T(8,128)(2,1)} async-done(((bf16[32,4096]{1,0:T(8,128)(2,1)}), bf16[16,4096]{1,0:T(8,128)(2,1)}) %reduce-scatter.19.cloned.1.call-update) | async-done | bytes 131088 | tf_op jit(solution)/shard_map/reduce_scatter | solution.py:169
  270.3 17.5 %reduce-scatter.15.cloned.1.call-done = bf16[16,4096]{1,0:T(8,128)(2,1)} async-done(((bf16[32,4096]{1,0:T(8,128)(2,1)}), bf16[16,4096]{1,0:T(8,128)(2,1)}) %reduce-scatter.15.cloned.1.call-update) | async-done | bytes 131088 | tf_op jit(solution)/shard_map/reduce_scatter | solution.py:169
  287.8 17.6 %reduce-scatter.11.cloned.1.call-done = bf16[16,4096]{1,0:T(8,128)(2,1)} async-done(((bf16[32,4096]{1,0:T(8,128)(2,1)}), bf16[16,4096]{1,0:T(8,128)(2,1)}) %reduce-scatter.11.cloned.1.call-update) | async-done | bytes 131088 | tf_op jit(solution)/shard_map/reduce_scatter | solution.py:169
  305.5 2.0 pad_maximum_fusion.1
  (49 shorter events, 3.0 us)
Async XLA Ops:
  7.2 4.8 %copy-start.1 = (s32[16]{0:T(128)S(1)}, s32[16]{0:T(128)}, u32[]{:S(2)}) copy-start(s32[16]{0:T(128)} %param.14) | copy-start | bytes 196
  7.2 52.1 %all-gather.2.cloned.1.call-start = ((), (), s32[]{:S(2)}) async-start(), calls=%async_computation.8 | async-start | bytes 4456448 | tf_op jit(solution)/shard_map/all_gather | solution.py:142
  12.1 4.0 %copy-start = (bf16[512,4096]{1,0:T(8,128)(2,1)S(1)}, bf16[512,4096]{1,0:T(8,128)(2,1)}, u32[]{:S(2)}) copy-start(bf16[512,4096]{1,0:T(8,128)(2,1)} %param.8) | copy-start | bytes 12582916
  20.7 189.9 %reduce-scatter.21.cloned.1.call-start = ((), (), s32[]{:S(2)}) async-start(), calls=%async_computation.15 | async-start | bytes 1310720 | tf_op jit(solution)/shard_map/reduce_scatter | solution.py:168
  94.9 116.2 %reduce-scatter.17.cloned.1.call-start = ((), (), s32[]{:S(2)}) async-start(), calls=%async_computation.13 | async-start | bytes 1310720 | tf_op jit(solution)/shard_map/reduce_scatter | solution.py:168
  133.2 78.7 %reduce-scatter.13.cloned.1.call-start = ((), (), s32[]{:S(2)}) async-start(), calls=%async_computation.11 | async-start | bytes 1310720 | tf_op jit(solution)/shard_map/reduce_scatter | solution.py:168
  171.8 63.4 %reduce-scatter.9.cloned.1.call-start = ((), (), s32[]{:S(2)}) async-start(), calls=%async_computation.9 | async-start | bytes 1310720 | tf_op jit(solution)/shard_map/reduce_scatter | solution.py:168
  206.5 28.7 %copy-start.2 = (s32[64]{0:T(128)S(1)}, s32[64]{0:T(128)}, u32[]{:S(2)}) copy-start(s32[64]{0:T(128)} %param.15) | copy-start | bytes 772
  210.5 42.2 %reduce-scatter.23.cloned.1.call-start = ((), (), s32[]{:S(2)}) async-start(), calls=%async_computation.16 | async-start | bytes 393216 | tf_op jit(solution)/shard_map/reduce_scatter | solution.py:169
  211.1 59.2 %reduce-scatter.19.cloned.1.call-start = ((), (), s32[]{:S(2)}) async-start(), calls=%async_computation.14 | async-start | bytes 393216 | tf_op jit(solution)/shard_map/reduce_scatter | solution.py:169
  211.8 76.0 %reduce-scatter.15.cloned.1.call-start = ((), (), s32[]{:S(2)}) async-start(), calls=%async_computation.12 | async-start | bytes 393216 | tf_op jit(solution)/shard_map/reduce_scatter | solution.py:169
  212.6 92.9 %reduce-scatter.11.cloned.1.call-start = ((), (), s32[]{:S(2)}) async-start(), calls=%async_computation.10 | async-start | bytes 393216 | tf_op jit(solution)/shard_map/reduce_scatter | solution.py:169
Sparse Core Ops, SparseCore 0:
  20.8 38.4 all-gather.1
  95.0 24.4 reduce-scatter.20
  133.3 24.4 reduce-scatter.16
  172.0 24.4 reduce-scatter.12
  210.6 24.5 reduce-scatter.8
  237.4 15.2 reduce-scatter.22
  255.2 15.1 reduce-scatter.18
  272.7 15.1 reduce-scatter.14
  290.3 15.1 reduce-scatter.10
